TPU v7x, 32 devices: a whole 2x2x4 slice. The times are simulated.
32 devices in a mesh: tm: 16 (over z, x, core), doc: 2 (over y).
Axes of the slice: x: 2, y: 2, z: 4, core: 2. Of those that a mesh axis runs over, the one named last changes fastest.
Arguments:
- beta: float32 [16, 4096, 128], P('tm', 'doc'), may hold values from -6 to 260
- word_ids: int32 [16, 8, 128], P('tm', 'doc'), may hold values from 0 to 4095
- word_counts: int32 [16, 8, 128], P('tm', 'doc'), may hold values from 1 to 8
- block_slot: int32 [32], replicated, may hold values from 0 to 31, each once
- topic_prior: float32 [128], replicated, may hold values from 0.05 to 0.5
- drift_var: float32 [128], replicated, may hold values from 0.0005 to 0.05
- obs_precision: float32 [16, 128], replicated, may hold values from 0.01 to 4
Outputs:
- smoothed_means: float32 [16, 4096, 128], P('tm', 'doc')
- doc_topics: float32 [16, 8, 128], P('tm', 'doc')
Inputs may be any that keep to these rules, and one draw needn't show every extreme that they name: `block_slot`: each block has its own position.
All inputs are finite; a program needn't handle non-finite values.
Results may differ from a plain program's by a relative error of at most 0.0012.
The roundings to bfloat16 on the way count: a program that leaves them out, or rounds other values in their place, can miss the bound.
Values may be sent and summed in bfloat16 or wider, within the bound.
No kernel may reach another device: no remote copies, remote signals or barrier semaphores. Data moves between devices by JAX's collectives and lax.ppermute only.
A program may use at most 192 MiB of HBM per device.

v0:
```python
import jax
import jax.numpy as jnp
from jax import lax
from jax.sharding import PartitionSpec as P

K = 128
BLOCK = 128
EITERS = 4
init_variance = 4.0


def variance_tables(obs_precision, drift_var):

    def forward_step(prior_var, precision):
        denominator = 1.0 + prior_var * precision
        gain_now = prior_var * precision / denominator
        filt_var = prior_var / denominator
        return (filt_var + drift_var, (gain_now, filt_var))

    start_var = jnp.full(drift_var.shape, init_variance, dtype=jnp.float32)
    last_var, (gains, filt_vars) = lax.scan(forward_step, start_var, obs_precision)

    def backward_step(info_next, precision):
        merged = info_next + precision
        shrink = 1.0 / (1.0 + drift_var * merged)
        info_now = merged * shrink
        return (info_now, (shrink, info_now))

    zero_info = jnp.zeros(drift_var.shape, dtype=jnp.float32)
    last_info, (shrinks, infos) = lax.scan(
        backward_step, zero_info, obs_precision[1:], reverse=True
    )
    shrinks = jnp.concatenate([shrinks, jnp.ones_like(zero_info)[None]], axis=0)
    infos = jnp.concatenate([infos, zero_info[None]], axis=0)
    return (gains, filt_vars, shrinks, infos)


def e_step(looked, word_counts, topic_prior):
    counts_float = word_counts.astype(jnp.float32)
    doc_topics = topic_prior + jnp.sum(counts_float, axis=-1, keepdims=True) / K
    scores = looked.astype(jnp.float32)
    for sweep in range(EITERS):
        resp = jax.nn.softmax(lax.digamma(doc_topics)[..., None, :] + scores, axis=-1)
        doc_topics = topic_prior + jnp.sum(counts_float[..., None] * resp, axis=-2)
    weighted = (counts_float[..., None] * resp).astype(jnp.bfloat16)
    return (doc_topics, weighted)


def body(beta, word_ids, word_counts, block_slot, topic_prior, drift_var, obs_precision):
    local_beta = beta[0]
    own_words = local_beta.shape[0]
    topics = local_beta.shape[1]
    doc_devices = lax.axis_size("doc")
    doc_place = lax.axis_index("doc")
    local_peak = jnp.max(local_beta, axis=0)
    local_total = jnp.sum(jnp.exp(local_beta - local_peak), axis=0)
    slot_ids = word_ids[0]
    local_docs = slot_ids.shape[0]
    slot_width = slot_ids.shape[1]
    columns = jnp.take(block_slot, slot_ids // BLOCK) * BLOCK + slot_ids % BLOCK
    all_columns = lax.all_gather(columns, "doc", axis=0, tiled=True)
    all_counts = lax.all_gather(word_counts[0], "doc", axis=0, tiled=True)
    peaks = lax.all_gather(local_peak, "doc")
    totals = lax.all_gather(local_total, "doc")
    peak_value = jnp.max(peaks, axis=0)
    total_value = jnp.sum(totals * jnp.exp(peaks - peak_value), axis=0)
    normalizer = peak_value + jnp.log(total_value)
    flat_columns = all_columns.reshape(-1)
    local_columns = flat_columns - doc_place * own_words
    inside = (local_columns >= 0) & (local_columns < own_words)
    picked = jnp.take(local_beta, jnp.clip(local_columns, 0, own_words - 1), axis=0)
    partial = jnp.where(
        inside[:, None], (picked - normalizer).astype(jnp.bfloat16), jnp.zeros((), jnp.bfloat16)
    )
    looked = lax.psum(partial, "doc").reshape(local_docs * doc_devices, slot_width, topics)
    doc_topics_all, weighted = e_step(looked, all_counts, topic_prior)
    doc_topics = lax.dynamic_slice_in_dim(doc_topics_all, doc_place * local_docs, local_docs, 0)
    flat_weighted = weighted.reshape(-1, topics)
    row_words = lax.iota(jnp.int32, own_words)
    marks = (row_words[:, None] == local_columns[None, :]).astype(jnp.bfloat16)
    counts = jnp.dot(marks, flat_weighted, preferred_element_type=jnp.float32)
    pseudo = local_beta + jnp.log1p(counts)
    gains, filt_vars, shrinks, infos = variance_tables(obs_precision, drift_var)
    years_total = obs_precision.shape[0]
    pulls = filt_vars / (filt_vars + drift_var)
    pulls = pulls.at[-1].set(0.0)
    years = lax.axis_size("tm")
    chunk = own_words // years
    by_year = lax.all_to_all(
        pseudo.reshape(years, chunk, topics), "tm", split_axis=0, concat_axis=0, tiled=True
    )

    def filter_step(mean_prev, inputs):
        gain_now, pseudo_now = inputs
        mean_now = (1.0 - gain_now) * mean_prev + gain_now * pseudo_now
        return (mean_now, mean_now)

    zero_mean = jnp.zeros((chunk, topics), dtype=jnp.float32)
    last_mean, filtered = lax.scan(
        filter_step, zero_mean, (gains[:, None, :], by_year), unroll=True
    )

    def smooth_step(mean_next, inputs):
        pull_now, filt_now = inputs
        mean_now = pull_now * mean_next + (1.0 - pull_now) * filt_now
        return (mean_now, mean_now)

    first_mean, smoothed = lax.scan(
        smooth_step, zero_mean, (pulls[:, None, :], filtered), reverse=True, unroll=True
    )
    back = lax.all_to_all(smoothed, "tm", split_axis=0, concat_axis=0, tiled=True)
    return (back.reshape(own_words, topics)[None], doc_topics[None])


def solution(mesh):
    in_specs = (
        P("tm", "doc", None),
        P("tm", "doc", None),
        P("tm", "doc", None),
        P(),
        P(),
        P(),
        P(),
    )
    out_specs = (P("tm", "doc", None), P("tm", "doc", None))
    return jax.shard_map(body, mesh=mesh, in_specs=in_specs, out_specs=out_specs, check_vma=False)
```

profile of v0, /device:TPU:9, one launch (start us, length us, event | category | flops | bytes accessed | tf_op | source)
XLA Modules:
  0.0 144.6 jit_solution(16217126004983186146)
XLA Ops:
  7.2 1.6 %reduce_max.54 = f32[128]{0:T(128)S(1)} reduce(f32[1,2048,128]{2,1,0:T(8,128)} %param.11, f32[]{:T(128)} %constant.154.clone.1), dimensions={0,1}, to_apply=%region_3.4 | reduce | flops 262016 | bytes 1049092 | tf_op jit(solution)/shard_map/reduce_max | solution.py:55
  8.8 0.3 exponential_reduce_fusion
  9.1 3.1 %all-gather.5 = f32[2,1,128]{2,1,0:T(1,128)S(1)} all-gather(f32[1,1,128]{2,1,0:T(1,128)S(1)} %bitcast.281), channel_id=4, replica_groups=mesh['tm'=16,'doc'=2] {'doc'}, dimensions={0}, use_global_device_ids=true | all-gather | bytes 1536 | tf_op jit(solution)/shard_map/all_gather | solution.py:64
  12.2 3.1 %all-gather.4 = f32[2,1,128]{2,1,0:T(1,128)S(1)} all-gather(f32[1,1,128]{2,1,0:T(1,128)S(1)} %bitcast.278), channel_id=3, replica_groups=mesh['tm'=16,'doc'=2] {'doc'}, dimensions={0}, use_global_device_ids=true | all-gather | bytes 1536 | tf_op jit(solution)/shard_map/all_gather | solution.py:63
  15.4 3.3 %gather_fusion = s32[512]{0:T(512)S(1)} fusion(s32[32]{0:T(128)S(1)} %copy-done, s32[1024]{0:T(1024)S(1)} %pad_clamp_fusion), kind=kCustom, calls=%fused_computation | custom fusion | bytes 6144 | tf_op jit(solution)/shard_map/jit(_take)/gather | solution.py:60
  18.8 3.2 %all-gather.3 = s32[2,4,128]{2,1,0:T(4,128)S(1)} all-gather(s32[1,4,128]{2,1,0:T(4,128)S(1)} %fusion.120), channel_id=1, replica_groups=mesh['tm'=16,'doc'=2] {'doc'}, dimensions={0}, use_global_device_ids=true | all-gather | bytes 6144 | tf_op jit(solution)/shard_map/all_gather | solution.py:61
  22.0 2.8 %gather_fusion.1 = f32[1024,128]{1,0:T(8,128)S(1)} fusion(f32[2048,128]{1,0:T(8,128)S(1)} %bitcast.257, s32[1024]{0:T(1024)S(1)} %broadcast_clamp_fusion), kind=kCustom, calls=%fused_computation.1 | custom fusion | bytes 1052672 | tf_op jit(solution)/shard_map/jit(_take)/gather | solution.py:71
  24.9 1.0 fusion.24
  25.9 3.2 %all-gather = s32[1,8,128]{2,0,1:T(1,128)S(1)} all-gather(s32[1,4,128]{2,0,1:T(1,128)S(1)} %bitcast.279), channel_id=2, replica_groups=mesh['tm'=16,'doc'=2] {'doc'}, dimensions={1}, use_global_device_ids=true | all-gather | bytes 6144 | tf_op jit(solution)/shard_map/all_gather | solution.py:62
  29.2 0.1 convert_reduce_fusion
  29.5 24.0 %all-reduce.2.cloned.1.call-done = bf16[1024,128]{1,0:T(8,128)(2,1)} async-done(((bf16[1024,128]{1,0:T(8,128)(2,1)}), bf16[1024,128]{1,0:T(8,128)(2,1)}) %all-reduce.2.cloned.1.call-update) | async-done | bytes 262160 | tf_op jit(solution)/shard_map/psum | solution.py:75
  53.5 1.2 fusion.6
  54.7 1.3 fusion.23
  56.1 1.4 multiply_reduce_fusion.3
  57.5 1.2 fusion.8
  58.7 0.4 fusion.21
  59.1 0.5 multiply_reduce_fusion.2
  59.7 0.2 fusion.10
  59.9 0.4 fusion.19
  60.3 0.5 multiply_reduce_fusion.1
  60.8 0.2 fusion.12
  61.1 0.4 fusion.15
  61.5 0.5 fusion.17
  61.9 2.8 %fusion.4 = f32[2048,128]{1,0:T(8,128)} fusion(bf16[1024,128]{1,0:T(8,128)(2,1)S(1)} %fusion.17, s32[1024]{0:T(1024)S(1)} %bitcast.274, f32[1,2048,128]{2,1,0:T(8,128)S(1)} %copy-done.2), kind=kOutput, calls=%fused_computation.11 | convolution fusion | flops 539230208 | bytes 2363392 | tf_op jit(solution)/shard_map/dot_general | solution.py:81
  64.7 7.0 %all-to-all-start = ((f32[16,128,128]{2,1,0:T(8,128)}), f32[16,128,128]{2,1,0:T(8,128)S(1)}, u32[]{:S(2)}, u32[]{:S(2)}) async-start(f32[16,128,128]{2,1,0:T(8,128)} %bitcast.59), calls=%async_computation | async-start | bytes 2097152 | tf_op jit(solution)/shard_map/all_to_all | solution.py:89
  71.7 12.5 %while.16 = (s32[]{:T(128)}, f32[128]{0:T(128)S(1)}, f32[16,128]{1,0:T(8,128)S(1)}, f32[16,128]{1,0:T(8,128)S(1)}, f32[16,128]{1,0:T(8,128)}, /*index=5*/f32[128]{0:T(128)S(1)}, s32[]{:T(128)}, s32[]{:T(128)}) while((s32[]{:T(128)}, f32[128]{0:T(128)S(1)}, f32[16,128]{1,0:T(8,128)S(1)}, f32[16,128]{1,0:T(8,128)S(1)}, ...), condition=%wide.region_1.0_spmd.clone, body=%wide.region_0.0_spmd.clone.sunk | while | flops 771 | bytes 5235 | solution.py:21
  71.7 0.7 fusion.137
  72.5 0.7 fusion.137
  73.3 0.7 fusion.137
  74.1 0.7 fusion.137
  74.8 0.7 fusion.137
  75.6 0.7 fusion.137
  76.4 0.7 fusion.137
  77.2 0.7 fusion.137
  78.0 0.7 fusion.137
  78.8 0.7 fusion.137
  79.5 0.7 fusion.137
  80.3 0.7 fusion.137
  81.1 0.7 fusion.137
  81.9 0.7 fusion.137
  82.7 0.7 fusion.137
  83.5 0.7 fusion.137
  84.3 12.3 %all-to-all-done = f32[16,128,128]{2,1,0:T(8,128)S(1)} async-done(((f32[16,128,128]{2,1,0:T(8,128)}), f32[16,128,128]{2,1,0:T(8,128)S(1)}, u32[]{:S(2)}, u32[]{:S(2)}) %all-to-all-start) | async-done | bytes 1048608 | tf_op jit(solution)/shard_map/all_to_all | solution.py:89
  96.6 0.9 add_dynamic-update-slice_fusion
  97.6 0.6 constant_dynamic-update-slice_fusion.13
  98.2 0.6 constant_dynamic-update-slice_fusion.12
  98.8 0.6 constant_dynamic-update-slice_fusion.11
  99.5 0.6 constant_dynamic-update-slice_fusion.10
  100.1 0.6 constant_dynamic-update-slice_fusion.9
  100.7 0.6 constant_dynamic-update-slice_fusion.8
  101.4 0.6 constant_dynamic-update-slice_fusion.7
  102.0 0.6 constant_dynamic-update-slice_fusion.6
  102.6 0.6 constant_dynamic-update-slice_fusion.5
  103.3 0.6 constant_dynamic-update-slice_fusion.4
  103.9 0.6 constant_dynamic-update-slice_fusion.3
  104.6 0.6 constant_dynamic-update-slice_fusion.2
  105.2 0.6 constant_dynamic-update-slice_fusion.1
  105.8 0.6 constant_dynamic-update-slice_fusion
  106.5 0.6 fusion.41
  107.1 4.8 %all-to-all-start.1 = ((f32[16,128,128]{2,1,0:T(8,128)}), f32[16,128,128]{2,1,0:T(8,128)S(1)}, u32[]{:S(2)}, u32[]{:S(2)}) async-start(f32[16,128,128]{2,1,0:T(8,128)} %fusion.41), calls=%async_computation.1 | async-start | bytes 2097152 | tf_op jit(solution)/shard_map/all_to_all | solution.py:111
  111.9 0.5 multiply_reduce_fusion
  112.4 0.6 dynamic-slice_bitcast_fusion
  113.0 23.8 %all-to-all-done.1 = f32[16,128,128]{2,1,0:T(8,128)S(1)} async-done(((f32[16,128,128]{2,1,0:T(8,128)}), f32[16,128,128]{2,1,0:T(8,128)S(1)}, u32[]{:S(2)}, u32[]{:S(2)}) %all-to-all-start.1) | async-done | bytes 1048608 | tf_op jit(solution)/shard_map/all_to_all | solution.py:111
  136.8 1.0 copy.43
  (73 shorter events, 1.5 us)
Async XLA Ops:
  7.2 8.2 %copy-start = (s32[32]{0:T(128)S(1)}, s32[32]{0:T(128)}, u32[]{:S(2)}) copy-start(s32[32]{0:T(128)} %param.14) | copy-start | bytes 388
  7.2 1.7 %copy-start.2 = (f32[1,2048,128]{2,1,0:T(8,128)S(1)}, f32[1,2048,128]{2,1,0:T(8,128)}, u32[]{:S(2)}) copy-start(f32[1,2048,128]{2,1,0:T(8,128)} %param.11) | copy-start | bytes 3145732
  7.2 46.3 %all-reduce.2.cloned.1.call-start = ((), (), s32[]{:S(2)}) async-start(), calls=%async_computation.2 | async-start | bytes 524288 | tf_op jit(solution)/shard_map/psum | solution.py:75
  7.2 8.1 %copy-start.5 = (s32[1,4,128]{2,1,0:T(4,128)S(1)}, s32[1,4,128]{2,1,0:T(4,128)}, u32[]{:S(2)}) copy-start(s32[1,4,128]{2,1,0:T(4,128)} %param.12) | copy-start | bytes 6148
  24.8 1.1 copy-start.6
  24.8 4.5 %copy-start.4 = (f32[128]{0:T(128)S(1)}, f32[128]{0:T(128)}, u32[]{:S(2)}) copy-start(f32[128]{0:T(128)} %param.15) | copy-start | bytes 1540
  53.5 5.2 %copy-start.1 = (bf16[1024,128]{1,0:T(8,128)(2,1)S(1)}, bf16[1024,128]{1,0:T(8,128)(2,1)}, u32[]{:S(2)}) copy-start(bf16[1024,128]{1,0:T(8,128)(2,1)} %all-reduce.2.cloned.1.call-done) | copy-start | bytes 786436
  64.7 7.0 %copy-start.3 = (f32[128]{0:T(128)S(1)}, f32[128]{0:T(128)}, u32[]{:S(2)}) copy-start(f32[128]{0:T(128)} %param.16) | copy-start | bytes 1540
  64.7 31.9 %all-to-all-start = ((f32[16,128,128]{2,1,0:T(8,128)}), f32[16,128,128]{2,1,0:T(8,128)S(1)}, u32[]{:S(2)}, u32[]{:S(2)}) async-start(f32[16,128,128]{2,1,0:T(8,128)} %bitcast.59), calls=%async_computation | async-start | bytes 2097152 | tf_op jit(solution)/shard_map/all_to_all | solution.py:89
  107.1 29.7 %all-to-all-start.1 = ((f32[16,128,128]{2,1,0:T(8,128)}), f32[16,128,128]{2,1,0:T(8,128)S(1)}, u32[]{:S(2)}, u32[]{:S(2)}) async-start(f32[16,128,128]{2,1,0:T(8,128)} %fusion.41), calls=%async_computation.1 | async-start | bytes 2097152 | tf_op jit(solution)/shard_map/all_to_all | solution.py:111
Sparse Core Ops, SparseCore 0:
  26.0 27.4 all-reduce.1
where the time goes:
time: 146 us; the launch traced here: 145 us
  waiting for transfers between devices  60.2 us (41%)
  other arithmetic  29.6 us (20%)
  between operations  14.3 us (10%)
  local copies, waits for them, and re-layouts  13.1 us (9%)
  blocking collectives  12.6 us (9%)
  starting transfers between devices  11.8 us (8%)
  matrix products  2.76 us (2%)
    psum x1, waiting for transfers between devices, body(): lax.psum(partial, 'doc')  24 us
    all_to_all x1, waiting for transfers between devices, body(): lax.all_to_all(smoothed, 'tm', split_axis=0, concat_axis=0, tiled=True)  23.8 us
    all_to_all x1, waiting for transfers between devices, body(): lax.all_to_all(pseudo.reshape(years, chunk, topics), 'tm', split_axis=0,...  12.3 us
    add x16, other arithmetic, forward_step(): return (filt_var + drift_var, (gain_now, filt_var))  11.4 us
    all_to_all x1, starting transfers between devices, body(): lax.all_to_all(pseudo.reshape(years, chunk, topics), 'tm', split_axis=0,...  6.99 us
    unnamed x22, local copies, waits for them, and re-layouts  5.44 us
    unnamed x10, other arithmetic  5.43 us
    all_to_all x1, starting transfers between devices, body(): lax.all_to_all(smoothed, 'tm', split_axis=0, concat_axis=0, tiled=True)  4.76 us
  transfers between devices with their start and end apart: 3, of which 3 were waited for; matrix products, arithmetic and copies ran while one was open for 9% of the time, Pallas kernels for 0%

commit v1 on v0

--- a/solution.py
+++ b/solution.py
@@ -58,7 +58,11 @@
     local_docs = slot_ids.shape[0]
     slot_width = slot_ids.shape[1]
     columns = jnp.take(block_slot, slot_ids // BLOCK) * BLOCK + slot_ids % BLOCK
-    all_columns = lax.all_gather(columns, "doc", axis=0, tiled=True)
+    count = lax.axis_size("doc")
+    repeats = [count if d == 0 else 1 for d in range(columns.ndim)]
+    all_columns = lax.all_to_all(
+        jnp.tile(columns, repeats), "doc", split_axis=0, concat_axis=0, tiled=True
+    )
     all_counts = lax.all_gather(word_counts[0], "doc", axis=0, tiled=True)
     peaks = lax.all_gather(local_peak, "doc")
     totals = lax.all_gather(local_total, "doc")

time: 146 us -> 149 us (1.021)
  waiting for transfers between devices: 60.2 us -> 64 us
  blocking collectives: 12.6 us -> 9.36 us
  starting transfers between devices: 11.8 us -> 15 us
    psum x1, waiting for transfers between devices: 24 us -> 27.8 us  [body(): lax.psum(partial, 'doc')]
    all_to_all x0 -> x1, starting transfers between devices: none -> 3.22 us  [body(): lax.all_to_all(jnp.tile(columns, repeats), 'doc', split_axis=0, concat_ax...]
    all_gather x1 -> x0, blocking collectives: 3.21 us -> none  [body(): all_columns = lax.all_gather(columns, 'doc', axis=0, tiled=True)]
    unnamed x10 -> x9, other arithmetic: 5.43 us -> 5.42 us
  transfers between devices with their start and end apart: 3 -> 4, of which waited for: 3 -> 3; matrix products, arithmetic and copies ran while one was open for 9% -> 10% of each run, Pallas kernels for 0% -> 0%
where the time goes in v1:
time: 149 us; the launch traced here: 148 us
  waiting for transfers between devices  64 us (43%)
  other arithmetic  29 us (19%)
  starting transfers between devices  15 us (10%)
  between operations  14.4 us (10%)
  local copies, waits for them, and re-layouts  13.7 us (9%)
  blocking collectives  9.36 us (6%)
  matrix products  2.76 us (2%)
    psum x1, waiting for transfers between devices, body(): lax.psum(partial, 'doc')  27.8 us
    all_to_all x1, waiting for transfers between devices, body(): lax.all_to_all(smoothed, 'tm', split_axis=0, concat_axis=0, tiled=True)  23.8 us
    all_to_all x1, waiting for transfers between devices, body(): lax.all_to_all(pseudo.reshape(years, chunk, topics), 'tm', split_axis=0,...  12.3 us
    add x16, other arithmetic, forward_step(): return (filt_var + drift_var, (gain_now, filt_var))  11.3 us
    all_to_all x1, starting transfers between devices, body(): lax.all_to_all(pseudo.reshape(years, chunk, topics), 'tm', split_axis=0,...  6.99 us
    unnamed x22, local copies, waits for them, and re-layouts  5.45 us
    unnamed x9, other arithmetic  5.42 us
    all_to_all x1, starting transfers between devices, body(): lax.all_to_all(smoothed, 'tm', split_axis=0, concat_axis=0, tiled=True)  4.76 us
  transfers between devices with their start and end apart: 4, of which 3 were waited for; matrix products, arithmetic and copies ran while one was open for 10% of the time, Pallas kernels for 0%

profile of v1, /device:TPU:9, one launch (start us, length us, event | category | flops | bytes accessed | tf_op | source)
XLA Modules:
  0.0 148.4 jit_solution(9539119454600555135)
XLA Ops:
  7.2 0.7 fusion.120
  7.9 3.3 %gather_fusion = s32[512]{0:T(512)S(1)} fusion(s32[32]{0:T(128)S(1)} %copy-done, s32[1024]{0:T(1024)S(1)} %pad_clamp_fusion), kind=kCustom, calls=%fused_computation | custom fusion | bytes 6144 | tf_op jit(solution)/shard_map/jit(_take)/gather | solution.py:60
  11.3 0.6 tile.2
  11.9 3.2 %all-to-all-start = ((s32[2,4,128]{2,1,0:T(4,128)}), s32[2,4,128]{2,1,0:T(4,128)S(1)}, u32[]{:S(2)}, u32[]{:S(2)}) async-start(s32[2,4,128]{2,1,0:T(4,128)} %tile.2), calls=%async_computation | async-start | bytes 8192 | tf_op jit(solution)/shard_map/all_to_all | solution.py:63
  15.2 0.3 reduce_max.54
  15.5 0.3 exponential_reduce_fusion
  15.8 3.1 %all-gather.4 = f32[2,1,128]{2,1,0:T(1,128)S(1)} all-gather(f32[1,1,128]{2,1,0:T(1,128)S(1)} %bitcast.279), channel_id=4, replica_groups=mesh['tm'=16,'doc'=2] {'doc'}, dimensions={0}, use_global_device_ids=true | all-gather | bytes 1536 | tf_op jit(solution)/shard_map/all_gather | solution.py:68
  18.9 3.1 %all-gather.3 = f32[2,1,128]{2,1,0:T(1,128)S(1)} all-gather(f32[1,1,128]{2,1,0:T(1,128)S(1)} %bitcast.276), channel_id=3, replica_groups=mesh['tm'=16,'doc'=2] {'doc'}, dimensions={0}, use_global_device_ids=true | all-gather | bytes 1536 | tf_op jit(solution)/shard_map/all_gather | solution.py:67
  22.0 3.2 %all-gather = s32[1,8,128]{2,0,1:T(1,128)S(1)} all-gather(s32[1,4,128]{2,0,1:T(1,128)S(1)} %bitcast.277), channel_id=2, replica_groups=mesh['tm'=16,'doc'=2] {'doc'}, dimensions={1}, use_global_device_ids=true | all-gather | bytes 6144 | tf_op jit(solution)/shard_map/all_gather | solution.py:66
  25.4 2.8 %gather_fusion.1 = f32[1024,128]{1,0:T(8,128)S(1)} fusion(f32[2048,128]{1,0:T(8,128)S(1)} %bitcast.255, s32[1024]{0:T(1024)S(1)} %broadcast_clamp_fusion), kind=kCustom, calls=%fused_computation.1 | custom fusion | bytes 1052672 | tf_op jit(solution)/shard_map/jit(_take)/gather | solution.py:75
  28.2 1.0 fusion.24
  29.5 27.8 %all-reduce.2.cloned.1.call-done = bf16[1024,128]{1,0:T(8,128)(2,1)} async-done(((bf16[1024,128]{1,0:T(8,128)(2,1)}), bf16[1024,128]{1,0:T(8,128)(2,1)}) %all-reduce.2.cloned.1.call-update) | async-done | bytes 262160 | tf_op jit(solution)/shard_map/psum | solution.py:79
  57.3 1.2 fusion.6
  58.5 1.3 fusion.23
  59.8 1.4 multiply_reduce_fusion.3
  61.3 1.2 fusion.8
  62.5 0.4 fusion.21
  62.9 0.5 multiply_reduce_fusion.2
  63.5 0.2 fusion.10
  63.7 0.4 fusion.19
  64.1 0.5 multiply_reduce_fusion.1
  64.9 0.4 fusion.15
  65.2 0.5 fusion.17
  65.7 2.8 %fusion.4 = f32[2048,128]{1,0:T(8,128)} fusion(bf16[1024,128]{1,0:T(8,128)(2,1)S(1)} %fusion.17, s32[1024]{0:T(1024)S(1)} %bitcast.272, f32[1,2048,128]{2,1,0:T(8,128)S(1)} %copy-done.2), kind=kOutput, calls=%fused_computation.11 | convolution fusion | flops 539230208 | bytes 2363392 | tf_op jit(solution)/shard_map/dot_general | solution.py:85
  68.5 7.0 %all-to-all-start.1 = ((f32[16,128,128]{2,1,0:T(8,128)}), f32[16,128,128]{2,1,0:T(8,128)S(1)}, u32[]{:S(2)}, u32[]{:S(2)}) async-start(f32[16,128,128]{2,1,0:T(8,128)} %bitcast.58), calls=%async_computation.1 | async-start | bytes 2097152 | tf_op jit(solution)/shard_map/all_to_all | solution.py:93
  75.5 12.5 %while.16 = (s32[]{:T(128)}, f32[128]{0:T(128)S(1)}, f32[16,128]{1,0:T(8,128)S(1)}, f32[16,128]{1,0:T(8,128)S(1)}, f32[16,128]{1,0:T(8,128)}, /*index=5*/f32[128]{0:T(128)S(1)}, s32[]{:T(128)}, s32[]{:T(128)}) while((s32[]{:T(128)}, f32[128]{0:T(128)S(1)}, f32[16,128]{1,0:T(8,128)S(1)}, f32[16,128]{1,0:T(8,128)S(1)}, ...), condition=%wide.region_1.0_spmd.clone, body=%wide.region_0.0_spmd.clone.sunk | while | flops 771 | bytes 5235 | solution.py:21
  75.5 0.7 fusion.136
  76.3 0.7 fusion.136
  77.1 0.7 fusion.136
  77.8 0.7 fusion.136
  78.6 0.7 fusion.136
  79.4 0.7 fusion.136
  80.2 0.7 fusion.136
  81.0 0.7 fusion.136
  81.8 0.7 fusion.136
  82.5 0.7 fusion.136
  83.3 0.7 fusion.136
  84.1 0.7 fusion.136
  84.9 0.7 fusion.136
  85.7 0.7 fusion.136
  86.4 0.7 fusion.136
  87.2 0.7 fusion.136
  88.1 12.3 %all-to-all-done.1 = f32[16,128,128]{2,1,0:T(8,128)S(1)} async-done(((f32[16,128,128]{2,1,0:T(8,128)}), f32[16,128,128]{2,1,0:T(8,128)S(1)}, u32[]{:S(2)}, u32[]{:S(2)}) %all-to-all-start.1) | async-done | bytes 1048608 | tf_op jit(solution)/shard_map/all_to_all | solution.py:93
  100.4 0.9 add_dynamic-update-slice_fusion
  101.3 0.6 constant_dynamic-update-slice_fusion.13
  102.0 0.6 constant_dynamic-update-slice_fusion.12
  102.6 0.6 constant_dynamic-update-slice_fusion.11
  103.3 0.6 constant_dynamic-update-slice_fusion.10
  103.9 0.6 constant_dynamic-update-slice_fusion.9
  104.5 0.6 constant_dynamic-update-slice_fusion.8
  105.2 0.6 constant_dynamic-update-slice_fusion.7
  105.8 0.6 constant_dynamic-update-slice_fusion.6
  106.4 0.6 constant_dynamic-update-slice_fusion.5
  107.1 0.6 constant_dynamic-update-slice_fusion.4
  107.7 0.6 constant_dynamic-update-slice_fusion.3
  108.4 0.6 constant_dynamic-update-slice_fusion.2
  109.0 0.6 constant_dynamic-update-slice_fusion.1
  109.6 0.6 constant_dynamic-update-slice_fusion
  110.3 0.6 fusion.41
  110.9 4.8 %all-to-all-start.2 = ((f32[16,128,128]{2,1,0:T(8,128)}), f32[16,128,128]{2,1,0:T(8,128)S(1)}, u32[]{:S(2)}, u32[]{:S(2)}) async-start(f32[16,128,128]{2,1,0:T(8,128)} %fusion.41), calls=%async_computation.2 | async-start | bytes 2097152 | tf_op jit(solution)/shard_map/all_to_all | solution.py:115
  115.7 0.5 multiply_reduce_fusion
  116.2 0.6 dynamic-slice_bitcast_fusion
  116.8 23.8 %all-to-all-done.2 = f32[16,128,128]{2,1,0:T(8,128)S(1)} async-done(((f32[16,128,128]{2,1,0:T(8,128)}), f32[16,128,128]{2,1,0:T(8,128)S(1)}, u32[]{:S(2)}, u32[]{:S(2)}) %all-to-all-start.2) | async-done | bytes 1048608 | tf_op jit(solution)/shard_map/all_to_all | solution.py:115
  140.6 1.0 copy.43
  (75 shorter events, 1.8 us)
Async XLA Ops:
  7.2 0.7 copy-start
  7.9 3.4 %copy-start.5 = (s32[1,4,128]{2,1,0:T(4,128)S(1)}, s32[1,4,128]{2,1,0:T(4,128)}, u32[]{:S(2)}) copy-start(s32[1,4,128]{2,1,0:T(4,128)} %param.12) | copy-start | bytes 6148
  7.9 7.3 %copy-start.2 = (f32[1,2048,128]{2,1,0:T(8,128)S(1)}, f32[1,2048,128]{2,1,0:T(8,128)}, u32[]{:S(2)}) copy-start(f32[1,2048,128]{2,1,0:T(8,128)} %param.11) | copy-start | bytes 3145732
  11.9 13.4 %all-to-all-start = ((s32[2,4,128]{2,1,0:T(4,128)}), s32[2,4,128]{2,1,0:T(4,128)S(1)}, u32[]{:S(2)}, u32[]{:S(2)}) async-start(s32[2,4,128]{2,1,0:T(4,128)} %tile.2), calls=%async_computation | async-start | bytes 8192 | tf_op jit(solution)/shard_map/all_to_all | solution.py:63
  15.1 6.9 %copy-start.6 = (s32[1,4,128]{2,1,0:T(4,128)S(1)}, s32[1,4,128]{2,1,0:T(4,128)}, u32[]{:S(2)}) copy-start(s32[1,4,128]{2,1,0:T(4,128)} %param.13) | copy-start | bytes 6148
  15.1 42.2 %all-reduce.2.cloned.1.call-start = ((), (), s32[]{:S(2)}) async-start(), calls=%async_computation.3 | async-start | bytes 524288 | tf_op jit(solution)/shard_map/psum | solution.py:79
  28.2 1.1 copy-start.4
  57.3 5.2 %copy-start.1 = (bf16[1024,128]{1,0:T(8,128)(2,1)S(1)}, bf16[1024,128]{1,0:T(8,128)(2,1)}, u32[]{:S(2)}) copy-start(bf16[1024,128]{1,0:T(8,128)(2,1)} %all-reduce.2.cloned.1.call-done) | copy-start | bytes 786436
  68.5 7.0 %copy-start.3 = (f32[128]{0:T(128)S(1)}, f32[128]{0:T(128)}, u32[]{:S(2)}) copy-start(f32[128]{0:T(128)} %param.16) | copy-start | bytes 1540
  68.5 31.9 %all-to-all-start.1 = ((f32[16,128,128]{2,1,0:T(8,128)}), f32[16,128,128]{2,1,0:T(8,128)S(1)}, u32[]{:S(2)}, u32[]{:S(2)}) async-start(f32[16,128,128]{2,1,0:T(8,128)} %bitcast.58), calls=%async_computation.1 | async-start | bytes 2097152 | tf_op jit(solution)/shard_map/all_to_all | solution.py:93
  110.9 29.7 %all-to-all-start.2 = ((f32[16,128,128]{2,1,0:T(8,128)}), f32[16,128,128]{2,1,0:T(8,128)S(1)}, u32[]{:S(2)}, u32[]{:S(2)}) async-start(f32[16,128,128]{2,1,0:T(8,128)} %fusion.41), calls=%async_computation.2 | async-start | bytes 2097152 | tf_op jit(solution)/shard_map/all_to_all | solution.py:115
Sparse Core Ops, SparseCore 0:
  29.4 27.8 all-reduce.1
